TPU v7x, 256 devices: a whole 4x4x8 slice. The times are simulated.
256 devices in a mesh: row: 8 (over x_hi, y), feat: 32 (over x_lo, z, core).
Axes of the slice: x: 4 (x_hi: 2, x_lo: 2; x = x_hi * 2 + x_lo), y: 4, z: 8, core: 2. Of those that a mesh axis runs over, the one named last changes fastest.
Arguments:
- node_features: bfloat16 [1024, 65536], P('feat', 'row'), may hold values from -6 to 6
- adjacency: bfloat16 [2048, 128, 128], P('row'), may hold values from -0.5 to 0.5
- tile_row: int32 [2048], P('row'), may hold values from 0 to 63
- tile_col: int32 [2048], P('row'), may hold values from 0 to 63
- tile_count: int32 [8, 8], P('row'), may hold values from 1 to 32, as said below
- weight: bfloat16 [1024, 1024], P('feat'), may hold values from -0.1875 to 0.1875
- out_bias: float32 [1024], replicated, may hold values from -3 to 3
Outputs:
- activated: bfloat16 [1024, 65536], P('feat', 'row')
Inputs may be any that keep to these rules, and one draw needn't show every extreme that they name: tile_count[r, s] is at least 1; the entry with s equal to r is 32.
All inputs are finite; a program needn't handle non-finite values.
Results may differ from a plain program's by a relative error of at most 0.0095.
Values may be sent and summed in bfloat16 or wider, within the bound.
No kernel may reach another device: no remote copies, remote signals or barrier semaphores. Data moves between devices by JAX's collectives and lax.ppermute only.
A program may use at most 128 MiB of HBM per device.

v0:
```python
import jax
import jax.numpy as jnp
from jax import lax
from jax.sharding import PartitionSpec as P


def from_behind(value, axis, steps):
    count = lax.axis_size(axis)
    pairs = [(source, (source + steps) % count) for source in range(count)]
    return lax.ppermute(value, axis, pairs)


def on_device(node_features, adjacency, tile_row, tile_col, tile_count, weight, out_bias):
    feat_width = node_features.shape[0]
    rows_here = node_features.shape[1]
    tile_size = adjacency.shape[1]
    row_blocks = rows_here // tile_size
    slot_total = tile_row.shape[0] // lax.axis_size("row")
    cycle_len = lax.axis_size("row")
    own_row = lax.axis_index("row")
    counts_here = tile_count[0]
    block_ids = jnp.arange(row_blocks)
    slot_ids = jnp.arange(slot_total)

    def add_source(running, held_block, source):
        first_slot = source * slot_total
        tiles_part = lax.dynamic_slice_in_dim(adjacency, first_slot, slot_total, 0)
        rows_part = lax.dynamic_slice_in_dim(tile_row, first_slot, slot_total, 0)
        cols_part = lax.dynamic_slice_in_dim(tile_col, first_slot, slot_total, 0)
        live_count = lax.dynamic_index_in_dim(counts_here, source, 0, keepdims=False)
        blocks = held_block.reshape(feat_width, row_blocks, tile_size)
        picked = jnp.take(blocks, cols_part, axis=1)
        product = jnp.einsum("fsj,sji->fsi", picked, tiles_part, preferred_element_type=jnp.float32)
        live_mask = slot_ids < live_count
        onehot = ((rows_part[:, None] == block_ids[None, :]) & live_mask[:, None]).astype(
            jnp.float32
        )
        return running + jnp.einsum("fsi,sr->fri", product, onehot)

    running = jnp.zeros((feat_width, row_blocks, tile_size), jnp.float32)
    running = add_source(running, node_features, own_row)
    held_block = node_features
    for step_num in range(1, cycle_len):
        held_block = from_behind(held_block, "row", 1)
        running = add_source(running, held_block, (own_row - step_num) % cycle_len)
    aggregated = running.reshape(feat_width, rows_here).astype(jnp.bfloat16)
    pre_act = jnp.dot(
        weight,
        lax.all_gather(aggregated, "feat", axis=0, tiled=True),
        preferred_element_type=jnp.float32,
    )
    bias_here = lax.dynamic_slice_in_dim(
        out_bias, lax.axis_index("feat") * feat_width, feat_width, 0
    )
    activated = jax.nn.relu(pre_act + bias_here[:, None]).astype(jnp.bfloat16)
    return activated


def solution(mesh):
    in_specs = (
        P("feat", "row"),
        P("row", None, None),
        P("row"),
        P("row"),
        P("row", None),
        P("feat", None),
        P(),
    )
    out_specs = P("feat", "row")
    return jax.shard_map(
        on_device, mesh=mesh, in_specs=in_specs, out_specs=out_specs, check_vma=False
    )
```

profile of v0, /device:TPU:1, one launch (start us, length us, event | category | flops | bytes accessed | tf_op | source)
XLA Modules:
  0.0 232.1 jit_solution(2701987297199606596)
XLA Ops:
  6.5 2.1 collective-permute-start
  8.7 1.2 copy_bitcast_fusion.8
  9.9 1.7 constant_dynamic-slice_fusion
  11.5 0.6 iota_compare_fusion.8
  12.7 0.6 iota_compare_fusion.11
  13.4 0.6 iota_compare_fusion.12
  14.0 0.6 iota_compare_fusion.13
  15.2 0.7 iota_compare_fusion.15
  16.0 1.1 fusion.109
  17.0 1.1 compare_and_fusion
  18.2 0.7 iota_compare_fusion.9
  19.5 1.7 convolution_bitcast_fusion.7
  21.6 0.9 collective-permute-done
  23.7 1.7 convolution_bitcast_fusion.6
  25.8 10.7 %collective-permute-done.1 = bf16[32,8192]{1,0:T(8,128)(2,1)S(1)} collective-permute-done((bf16[32,8192]{1,0:T(8,128)(2,1)S(1)}, bf16[32,8192]{1,0:T(8,128)(2,1)S(1)}, u32[]{:S(2)}, u32[]{:S(2)}) %collective-permute-start.1) | collective-permute-done | bytes 524320 | tf_op jit(solution)/shard_map/ppermute | solution.py:10
  37.2 1.7 convolution_bitcast_fusion.5
  39.3 10.3 %collective-permute-done.2 = bf16[32,8192]{1,0:T(8,128)(2,1)S(1)} collective-permute-done((bf16[32,8192]{1,0:T(8,128)(2,1)S(1)}, bf16[32,8192]{1,0:T(8,128)(2,1)S(1)}, u32[]{:S(2)}, u32[]{:S(2)}) %collective-permute-start.2) | collective-permute-done | bytes 524320 | tf_op jit(solution)/shard_map/ppermute | solution.py:10
  50.3 1.7 convolution_bitcast_fusion.4
  52.4 9.5 %collective-permute-done.3 = bf16[32,8192]{1,0:T(8,128)(2,1)S(1)} collective-permute-done((bf16[32,8192]{1,0:T(8,128)(2,1)S(1)}, bf16[32,8192]{1,0:T(8,128)(2,1)S(1)}, u32[]{:S(2)}, u32[]{:S(2)}) %collective-permute-start.3) | collective-permute-done | bytes 524320 | tf_op jit(solution)/shard_map/ppermute | solution.py:10
  62.6 1.7 convolution_bitcast_fusion.3
  64.7 8.8 %collective-permute-done.4 = bf16[32,8192]{1,0:T(8,128)(2,1)S(1)} collective-permute-done((bf16[32,8192]{1,0:T(8,128)(2,1)S(1)}, bf16[32,8192]{1,0:T(8,128)(2,1)S(1)}, u32[]{:S(2)}, u32[]{:S(2)}) %collective-permute-start.4) | collective-permute-done | bytes 524320 | tf_op jit(solution)/shard_map/ppermute | solution.py:10
  73.6 0.6 gather_fusion.5
  74.2 1.7 convolution_bitcast_fusion.2
  76.3 9.0 %collective-permute-done.5 = bf16[32,8192]{1,0:T(8,128)(2,1)S(1)} collective-permute-done((bf16[32,8192]{1,0:T(8,128)(2,1)S(1)}, bf16[32,8192]{1,0:T(8,128)(2,1)S(1)}, u32[]{:S(2)}, u32[]{:S(2)}) %collective-permute-start.5) | collective-permute-done | bytes 524320 | tf_op jit(solution)/shard_map/ppermute | solution.py:10
  85.4 0.6 gather_fusion.6
  86.0 1.7 convolution_bitcast_fusion.1
  88.1 10.1 %collective-permute-done.6 = bf16[32,8192]{1,0:T(8,128)(2,1)S(1)} collective-permute-done((bf16[32,8192]{1,0:T(8,128)(2,1)S(1)}, bf16[32,8192]{1,0:T(8,128)(2,1)S(1)}, u32[]{:S(2)}, u32[]{:S(2)}) %collective-permute-start.6) | collective-permute-done | bytes 524320 | tf_op jit(solution)/shard_map/ppermute | solution.py:10
  98.9 1.7 convolution_bitcast_fusion
  101.0 1.1 copy.58
  102.2 0.8 dynamic_slice.132
  102.9 112.8 %all-gather.2.cloned.1.call-done = bf16[1024,8192]{1,0:T(8,128)(2,1)} async-done(((bf16[32,8192]{1,0:T(8,128)(2,1)}), bf16[1024,8192]{1,0:T(8,128)(2,1)}) %all-gather.2.cloned.1.call-update) | async-done | bytes 16777232 | tf_op jit(solution)/shard_map/all_gather | solution.py:49
  215.8 9.6 %fusion.2 = bf16[32,8192]{1,0:T(8,128)(2,1)} fusion(bf16[32,1024]{1,0:T(8,128)(2,1)S(1)} %copy-done, bf16[1024,8192]{1,0:T(8,128)(2,1)} %all-gather.2.cloned.1.call-done, f32[32]{0:T(128)S(1)} %dynamic_slice.132), kind=kOutput, calls=%fused_computation.11 | convolution fusion | flops 537657344 | bytes 17367168 | tf_op jit(solution)/shard_map/dot_general | solution.py:47
  (41 shorter events, 9.3 us)
Async XLA Ops:
  6.5 209.2 %copy-start = (bf16[32,1024]{1,0:T(8,128)(2,1)S(1)}, bf16[32,1024]{1,0:T(8,128)(2,1)}, u32[]{:S(2)}) copy-start(bf16[32,1024]{1,0:T(8,128)(2,1)} %param.14) | copy-start | bytes 196612
  6.5 209.2 %all-gather.2.cloned.1.call-start = ((), (), s32[]{:S(2)}) async-start(), calls=%async_computation | async-start | bytes 17301504 | tf_op jit(solution)/shard_map/all_gather | solution.py:49
  6.5 16.0 %collective-permute-start = (bf16[32,8192]{1,0:T(8,128)(2,1)}, bf16[32,8192]{1,0:T(8,128)(2,1)S(1)}, u32[]{:S(2)}, u32[]{:S(2)}) collective-permute-start(bf16[32,8192]{1,0:T(8,128)(2,1)} %param.9), channel_id=1, source_target_pairs={{0,32},{32,64},{64,96},{96,128},{128,160},{160,192},{192,224},{224... | collective-permute-start | bytes 1572872 | tf_op jit(solution)/shard_map/ppermute | solution.py:10
  22.5 14.0 %collective-permute-start.1 = (bf16[32,8192]{1,0:T(8,128)(2,1)S(1)}, bf16[32,8192]{1,0:T(8,128)(2,1)S(1)}, u32[]{:S(2)}, u32[]{:S(2)}) collective-permute-start(bf16[32,8192]{1,0:T(8,128)(2,1)S(1)} %collective-permute-done), channel_id=1, source_target_pairs={{0,32},{32,64},{64,96},{96,128},{128,160},{160,192},{192,224},{224... | collective-permute-start | bytes 1572872 | tf_op jit(solution)/shard_map/ppermute | solution.py:10
  36.5 13.1 %collective-permute-start.2 = (bf16[32,8192]{1,0:T(8,128)(2,1)S(1)}, bf16[32,8192]{1,0:T(8,128)(2,1)S(1)}, u32[]{:S(2)}, u32[]{:S(2)}) collective-permute-start(bf16[32,8192]{1,0:T(8,128)(2,1)S(1)} %collective-permute-done.1), channel_id=1, source_target_pairs={{0,32},{32,64},{64,96},{96,128},{128,160},{160,192},{192,224},{224... | collective-permute-start | bytes 1572872 | tf_op jit(solution)/shard_map/ppermute | solution.py:10
  49.6 12.3 %collective-permute-start.3 = (bf16[32,8192]{1,0:T(8,128)(2,1)S(1)}, bf16[32,8192]{1,0:T(8,128)(2,1)S(1)}, u32[]{:S(2)}, u32[]{:S(2)}) collective-permute-start(bf16[32,8192]{1,0:T(8,128)(2,1)S(1)} %collective-permute-done.2), channel_id=1, source_target_pairs={{0,32},{32,64},{64,96},{96,128},{128,160},{160,192},{192,224},{224... | collective-permute-start | bytes 1572872 | tf_op jit(solution)/shard_map/ppermute | solution.py:10
  61.9 11.6 %collective-permute-start.4 = (bf16[32,8192]{1,0:T(8,128)(2,1)S(1)}, bf16[32,8192]{1,0:T(8,128)(2,1)S(1)}, u32[]{:S(2)}, u32[]{:S(2)}) collective-permute-start(bf16[32,8192]{1,0:T(8,128)(2,1)S(1)} %collective-permute-done.3), channel_id=1, source_target_pairs={{0,32},{32,64},{64,96},{96,128},{128,160},{160,192},{192,224},{224... | collective-permute-start | bytes 1572872 | tf_op jit(solution)/shard_map/ppermute | solution.py:10
  73.5 11.8 %collective-permute-start.5 = (bf16[32,8192]{1,0:T(8,128)(2,1)S(1)}, bf16[32,8192]{1,0:T(8,128)(2,1)S(1)}, u32[]{:S(2)}, u32[]{:S(2)}) collective-permute-start(bf16[32,8192]{1,0:T(8,128)(2,1)S(1)} %collective-permute-done.4), channel_id=1, source_target_pairs={{0,32},{32,64},{64,96},{96,128},{128,160},{160,192},{192,224},{224... | collective-permute-start | bytes 1572872 | tf_op jit(solution)/shard_map/ppermute | solution.py:10
  85.3 12.9 %collective-permute-start.6 = (bf16[32,8192]{1,0:T(8,128)(2,1)S(1)}, bf16[32,8192]{1,0:T(8,128)(2,1)S(1)}, u32[]{:S(2)}, u32[]{:S(2)}) collective-permute-start(bf16[32,8192]{1,0:T(8,128)(2,1)S(1)} %collective-permute-done.5), channel_id=1, source_target_pairs={{0,32},{32,64},{64,96},{96,128},{128,160},{160,192},{192,224},{224... | collective-permute-start | bytes 1572872 | tf_op jit(solution)/shard_map/ppermute | solution.py:10
Sparse Core Ops, SparseCore 0:
  102.3 113.4 all-gather.1
where the time goes:
time: 233 us; the launch traced here: 232 us
  waiting for transfers between devices  172 us (74%)
  matrix products  26.3 us (11%)
  between operations  13.8 us (6%)
  local copies, waits for them, and re-layouts  11.2 us (5%)
  other arithmetic  6.17 us (3%)
  starting transfers between devices  2.62 us (1%)
    all_gather x1, waiting for transfers between devices, on_device(): lax.all_gather(aggregated, 'feat', axis=0, tiled=True)  113 us
    ppermute x7, waiting for transfers between devices, from_behind(): return lax.ppermute(value, axis, pairs)  59.2 us
    dot_general x8, matrix products, add_source(): jnp.einsum('fsj,sji->fsi', picked, tiles_part, preferred_element_type=jnp...  13.3 us
    dot_general x1, matrix products, on_device(): jnp.dot(weight, lax.all_gather(aggregated, 'feat', axis=0, tiled=True), p...  9.55 us
    lt x8, other arithmetic, add_source(): live_mask = slot_ids < live_count  5.05 us
    gather x8, local copies, waits for them, and re-layouts, add_source(): picked = jnp.take(blocks, cols_part, axis=1)  4.82 us
  transfers between devices with their start and end apart: 8, of which 8 were waited for; matrix products, arithmetic and copies ran while one was open for 13% of the time, Pallas kernels for 0%

commit v1 on v0

--- a/solution.py
+++ b/solution.py
@@ -46,7 +46,9 @@
     aggregated = running.reshape(feat_width, rows_here).astype(jnp.bfloat16)
     pre_act = jnp.dot(
         weight,
-        lax.all_gather(aggregated, "feat", axis=0, tiled=True),
+        jnp.concatenate(
+            lax.all_to_all(jnp.stack([aggregated] * lax.axis_size("feat")), "feat", 0, 0), axis=0
+        ),
         preferred_element_type=jnp.float32,
     )
     bias_here = lax.dynamic_slice_in_dim(

time: 233 us -> 505 us (2.17); the launches traced: 232 us -> 495 us
  waiting for transfers between devices: 172 us -> 420 us
  starting transfers between devices: 2.62 us -> 25.8 us
  between operations: 13.8 us -> 0.42 us
  local copies, waits for them, and re-layouts: 11.2 us -> 16.4 us
    all_to_all x0 -> x1, waiting for transfers between devices: none -> 360 us  [on_device(): lax.all_to_all(jnp.stack([aggregated] * lax.axis_size('feat')), 'feat', 0...]
    all_gather x1 -> x0, waiting for transfers between devices: 113 us -> none  [on_device(): lax.all_gather(aggregated, 'feat', axis=0, tiled=True)]
    all_to_all x0 -> x1, starting transfers between devices: none -> 23.3 us  [on_device(): lax.all_to_all(jnp.stack([aggregated] * lax.axis_size('feat')), 'feat', 0...]
    another operation x0 -> x1, local copies, waits for them, and re-layouts: none -> 5.96 us  [on_device(): jnp.stack([aggregated] * lax.axis_size('feat'))]
  transfers between devices with their start and end apart: 8 -> 8, of which waited for: 8 -> 8; matrix products, arithmetic and copies ran while one was open for 13% -> 6% of each run, Pallas kernels for 0% -> 0%
where the time goes in v1:
time: 505 us; the launch traced here: 495 us
  waiting for transfers between devices  420 us (83%)
  matrix products  26.3 us (5%)
  starting transfers between devices  25.8 us (5%)
  local copies, waits for them, and re-layouts  16.4 us (3%)
  other arithmetic  6.12 us (1%)
    all_to_all x1, waiting for transfers between devices, on_device(): lax.all_to_all(jnp.stack([aggregated] * lax.axis_size('feat')), 'feat', 0...  360 us
    ppermute x7, waiting for transfers between devices, from_behind(): return lax.ppermute(value, axis, pairs)  59.3 us
    all_to_all x1, starting transfers between devices, on_device(): lax.all_to_all(jnp.stack([aggregated] * lax.axis_size('feat')), 'feat', 0...  23.3 us
    dot_general x8, matrix products, add_source(): jnp.einsum('fsj,sji->fsi', picked, tiles_part, preferred_element_type=jnp...  13.3 us
  transfers between devices with their start and end apart: 8, of which 8 were waited for; matrix products, arithmetic and copies ran while one was open for 6% of the time, Pallas kernels for 0%

profile of v1, /device:TPU:1, one launch (start us, length us, event | category | flops | bytes accessed | tf_op | source)
XLA Modules:
  0.0 494.8 jit_solution(3389323802859677803)
XLA Ops:
  0.0 2.1 collective-permute-start
  2.1 1.2 copy_bitcast_fusion.8
  3.3 1.7 constant_dynamic-slice_fusion
  5.0 0.6 iota_compare_fusion.8
  5.6 0.6 iota_compare_fusion.10
  6.9 0.6 iota_compare_fusion.12
  7.5 0.6 iota_compare_fusion.13
  8.1 0.6 iota_compare_fusion.14
  9.4 1.1 fusion.109
  10.4 1.1 compare_and_fusion
  11.6 0.7 iota_compare_fusion.9
  12.9 1.7 convolution_bitcast_fusion.7
  15.0 0.9 collective-permute-done
  16.5 0.6 gather_fusion.1
  17.1 1.7 convolution_bitcast_fusion.6
  19.2 10.7 %collective-permute-done.1 = bf16[32,8192]{1,0:T(8,128)(2,1)S(1)} collective-permute-done((bf16[32,8192]{1,0:T(8,128)(2,1)S(1)}, bf16[32,8192]{1,0:T(8,128)(2,1)S(1)}, u32[]{:S(2)}, u32[]{:S(2)}) %collective-permute-start.1) | collective-permute-done | bytes 524320 | tf_op jit(solution)/shard_map/ppermute | solution.py:10
  30.7 1.7 convolution_bitcast_fusion.5
  32.8 10.3 %collective-permute-done.2 = bf16[32,8192]{1,0:T(8,128)(2,1)S(1)} collective-permute-done((bf16[32,8192]{1,0:T(8,128)(2,1)S(1)}, bf16[32,8192]{1,0:T(8,128)(2,1)S(1)}, u32[]{:S(2)}, u32[]{:S(2)}) %collective-permute-start.2) | collective-permute-done | bytes 524320 | tf_op jit(solution)/shard_map/ppermute | solution.py:10
  43.8 1.7 convolution_bitcast_fusion.4
  45.9 9.5 %collective-permute-done.3 = bf16[32,8192]{1,0:T(8,128)(2,1)S(1)} collective-permute-done((bf16[32,8192]{1,0:T(8,128)(2,1)S(1)}, bf16[32,8192]{1,0:T(8,128)(2,1)S(1)}, u32[]{:S(2)}, u32[]{:S(2)}) %collective-permute-start.3) | collective-permute-done | bytes 524320 | tf_op jit(solution)/shard_map/ppermute | solution.py:10
  56.0 1.7 convolution_bitcast_fusion.3
  58.1 8.8 %collective-permute-done.4 = bf16[32,8192]{1,0:T(8,128)(2,1)S(1)} collective-permute-done((bf16[32,8192]{1,0:T(8,128)(2,1)S(1)}, bf16[32,8192]{1,0:T(8,128)(2,1)S(1)}, u32[]{:S(2)}, u32[]{:S(2)}) %collective-permute-start.4) | collective-permute-done | bytes 524320 | tf_op jit(solution)/shard_map/ppermute | solution.py:10
  67.7 1.7 convolution_bitcast_fusion.2
  69.8 9.0 %collective-permute-done.5 = bf16[32,8192]{1,0:T(8,128)(2,1)S(1)} collective-permute-done((bf16[32,8192]{1,0:T(8,128)(2,1)S(1)}, bf16[32,8192]{1,0:T(8,128)(2,1)S(1)}, u32[]{:S(2)}, u32[]{:S(2)}) %collective-permute-start.5) | collective-permute-done | bytes 524320 | tf_op jit(solution)/shard_map/ppermute | solution.py:10
  79.5 1.7 convolution_bitcast_fusion.1
  81.6 10.1 %collective-permute-done.6 = bf16[32,8192]{1,0:T(8,128)(2,1)S(1)} collective-permute-done((bf16[32,8192]{1,0:T(8,128)(2,1)S(1)}, bf16[32,8192]{1,0:T(8,128)(2,1)S(1)}, u32[]{:S(2)}, u32[]{:S(2)}) %collective-permute-start.6) | collective-permute-done | bytes 524320 | tf_op jit(solution)/shard_map/ppermute | solution.py:10
  92.4 1.7 convolution_bitcast_fusion
  94.8 6.0 %stack.2 = bf16[32,32,8192]{2,1,0:T(8,128)(2,1)} broadcast(bf16[32,8192]{1,0:T(8,128)(2,1)S(1)} %bitcast.123), dimensions={1,2} | broadcast | bytes 17301504 | tf_op jit(solution)/shard_map/stack | solution.py:50
  100.8 23.3 %all-to-all-start = ((bf16[32,32,8192]{2,1,0:T(8,128)(2,1)}), bf16[32,32,8192]{2,1,0:T(8,128)(2,1)}, u32[]{:S(2)}, u32[]{:S(2)}) async-start(bf16[32,32,8192]{2,1,0:T(8,128)(2,1)} %stack.2), calls=%async_computation | async-start | bytes 33554432 | tf_op jit(solution)/shard_map/all_to_all | solution.py:50
  124.1 0.8 dynamic_slice.132
  124.8 360.4 %all-to-all-done = bf16[32,32,8192]{2,1,0:T(8,128)(2,1)} async-done(((bf16[32,32,8192]{2,1,0:T(8,128)(2,1)}), bf16[32,32,8192]{2,1,0:T(8,128)(2,1)}, u32[]{:S(2)}, u32[]{:S(2)}) %all-to-all-start) | async-done | bytes 16777248 | tf_op jit(solution)/shard_map/all_to_all | solution.py:50
  485.3 9.6 %fusion.2 = bf16[32,8192]{1,0:T(8,128)(2,1)} fusion(bf16[32,1024]{1,0:T(8,128)(2,1)S(1)} %copy-done, bf16[1024,8192]{1,0:T(8,128)(2,1)} %bitcast.33, f32[32]{0:T(128)S(1)} %dynamic_slice.132), kind=kOutput, calls=%fused_computation.11 | convolution fusion | flops 537657344 | bytes 17367168 | tf_op jit(solution)/shard_map/dot_general | solution.py:47
  (41 shorter events, 10.2 us)
Async XLA Ops:
  0.0 485.2 %copy-start = (bf16[32,1024]{1,0:T(8,128)(2,1)S(1)}, bf16[32,1024]{1,0:T(8,128)(2,1)}, u32[]{:S(2)}) copy-start(bf16[32,1024]{1,0:T(8,128)(2,1)} %param.14) | copy-start | bytes 196612
  0.0 16.0 %collective-permute-start = (bf16[32,8192]{1,0:T(8,128)(2,1)}, bf16[32,8192]{1,0:T(8,128)(2,1)S(1)}, u32[]{:S(2)}, u32[]{:S(2)}) collective-permute-start(bf16[32,8192]{1,0:T(8,128)(2,1)} %param.9), channel_id=1, source_target_pairs={{0,32},{32,64},{64,96},{96,128},{128,160},{160,192},{192,224},{224... | collective-permute-start | bytes 1572872 | tf_op jit(solution)/shard_map/ppermute | solution.py:10
  16.0 14.0 %collective-permute-start.1 = (bf16[32,8192]{1,0:T(8,128)(2,1)S(1)}, bf16[32,8192]{1,0:T(8,128)(2,1)S(1)}, u32[]{:S(2)}, u32[]{:S(2)}) collective-permute-start(bf16[32,8192]{1,0:T(8,128)(2,1)S(1)} %collective-permute-done), channel_id=1, source_target_pairs={{0,32},{32,64},{64,96},{96,128},{128,160},{160,192},{192,224},{224... | collective-permute-start | bytes 1572872 | tf_op jit(solution)/shard_map/ppermute | solution.py:10
  30.0 13.1 %collective-permute-start.2 = (bf16[32,8192]{1,0:T(8,128)(2,1)S(1)}, bf16[32,8192]{1,0:T(8,128)(2,1)S(1)}, u32[]{:S(2)}, u32[]{:S(2)}) collective-permute-start(bf16[32,8192]{1,0:T(8,128)(2,1)S(1)} %collective-permute-done.1), channel_id=1, source_target_pairs={{0,32},{32,64},{64,96},{96,128},{128,160},{160,192},{192,224},{224... | collective-permute-start | bytes 1572872 | tf_op jit(solution)/shard_map/ppermute | solution.py:10
  43.1 12.3 %collective-permute-start.3 = (bf16[32,8192]{1,0:T(8,128)(2,1)S(1)}, bf16[32,8192]{1,0:T(8,128)(2,1)S(1)}, u32[]{:S(2)}, u32[]{:S(2)}) collective-permute-start(bf16[32,8192]{1,0:T(8,128)(2,1)S(1)} %collective-permute-done.2), channel_id=1, source_target_pairs={{0,32},{32,64},{64,96},{96,128},{128,160},{160,192},{192,224},{224... | collective-permute-start | bytes 1572872 | tf_op jit(solution)/shard_map/ppermute | solution.py:10
  55.3 11.6 %collective-permute-start.4 = (bf16[32,8192]{1,0:T(8,128)(2,1)S(1)}, bf16[32,8192]{1,0:T(8,128)(2,1)S(1)}, u32[]{:S(2)}, u32[]{:S(2)}) collective-permute-start(bf16[32,8192]{1,0:T(8,128)(2,1)S(1)} %collective-permute-done.3), channel_id=1, source_target_pairs={{0,32},{32,64},{64,96},{96,128},{128,160},{160,192},{192,224},{224... | collective-permute-start | bytes 1572872 | tf_op jit(solution)/shard_map/ppermute | solution.py:10
  67.0 11.8 %collective-permute-start.5 = (bf16[32,8192]{1,0:T(8,128)(2,1)S(1)}, bf16[32,8192]{1,0:T(8,128)(2,1)S(1)}, u32[]{:S(2)}, u32[]{:S(2)}) collective-permute-start(bf16[32,8192]{1,0:T(8,128)(2,1)S(1)} %collective-permute-done.4), channel_id=1, source_target_pairs={{0,32},{32,64},{64,96},{96,128},{128,160},{160,192},{192,224},{224... | collective-permute-start | bytes 1572872 | tf_op jit(solution)/shard_map/ppermute | solution.py:10
  78.8 12.9 %collective-permute-start.6 = (bf16[32,8192]{1,0:T(8,128)(2,1)S(1)}, bf16[32,8192]{1,0:T(8,128)(2,1)S(1)}, u32[]{:S(2)}, u32[]{:S(2)}) collective-permute-start(bf16[32,8192]{1,0:T(8,128)(2,1)S(1)} %collective-permute-done.5), channel_id=1, source_target_pairs={{0,32},{32,64},{64,96},{96,128},{128,160},{160,192},{192,224},{224... | collective-permute-start | bytes 1572872 | tf_op jit(solution)/shard_map/ppermute | solution.py:10
  100.8 384.5 %all-to-all-start = ((bf16[32,32,8192]{2,1,0:T(8,128)(2,1)}), bf16[32,32,8192]{2,1,0:T(8,128)(2,1)}, u32[]{:S(2)}, u32[]{:S(2)}) async-start(bf16[32,32,8192]{2,1,0:T(8,128)(2,1)} %stack.2), calls=%async_computation | async-start | bytes 33554432 | tf_op jit(solution)/shard_map/all_to_all | solution.py:50
